TPU v7x, 512 devices: a whole 4x4x16 slice. The times are simulated.
512 devices in a mesh: seq: 64 (over z, y), tp: 8 (over x, core).
Axes of the slice: x: 4, y: 4, z: 16, core: 2. Of those that a mesh axis runs over, the one named last changes fastest.
Arguments:
- cache: bfloat16 [2, 64, 512, 3072], P(None, 'seq', 'tp'), may hold values from -24 to 24
- cache_len: int32 [64], replicated, may hold values from 1 to 512, 16384 in all
- group: bfloat16 [3, 64, 256, 3072], P(None, 'seq', None, 'tp'), may hold values from -24 to 24
- group_req: int32 [64], replicated, may hold values from 0 to 63, each once
- req_order: int32 [64], replicated, may hold values from 0 to 63, each once
Outputs:
- context: bfloat16 [64, 256, 3072], P('seq', None, 'tp')
Inputs may be any that keep to these rules, and one draw needn't show every extreme that they name: `group_req`: each request once. `req_order`: each request once.
All inputs are finite; a program needn't handle non-finite values.
Results may differ from a plain program's by a relative error of at most 0.0042.
Values may be sent and summed in bfloat16 or wider, within the bound.
No kernel may reach another device: no remote copies, remote signals or barrier semaphores. Data moves between devices by JAX's collectives and lax.ppermute only.
A program may use at most 64 MiB of HBM per device.

v0:
```python
import math
import jax
import jax.numpy as jnp
from jax import lax
from jax.sharding import PartitionSpec as P

HD = 96


def inverse_table(permutation):
    numbers = jnp.arange(permutation.shape[0], dtype=jnp.int32)
    matches = permutation[None, :] == numbers[:, None]
    return jnp.sum(jnp.where(matches, numbers[None, :], 0), axis=1)


def partial_part(queries, key_rows, value_rows, keep, factor):
    scores = (
        jnp.einsum("qhd,khd->hqk", queries, key_rows, preferred_element_type=jnp.float32) * factor
    )
    scores = jnp.where(keep[None], scores, -jnp.inf)
    row_top = jnp.max(scores, axis=-1)
    weights = jnp.exp(scores - row_top[..., None]).astype(jnp.bfloat16)
    weight_sum = jnp.sum(weights, axis=-1, dtype=jnp.float32)
    weighted = jnp.einsum("hqk,khd->hqd", weights, value_rows, preferred_element_type=jnp.float32)
    return (row_top, weight_sum, weighted)


def combine_parts(first_part, second_part):
    top_one, sum_one, mixed_one = first_part
    top_two, sum_two, mixed_two = second_part
    row_top = jnp.maximum(top_one, top_two)
    factor_one = jnp.exp(top_one - row_top)
    factor_two = jnp.exp(top_two - row_top)
    result = (factor_one[..., None] * mixed_one + factor_two[..., None] * mixed_two) / (
        factor_one * sum_one + factor_two * sum_two
    )[..., None]
    result = jnp.transpose(result, (1, 0, 2))
    return result.reshape(result.shape[0], -1).astype(jnp.bfloat16)


def permute_rows(rows, order):
    count = order.shape[0]
    pieces = rows.reshape(count, rows.shape[0] // count, rows.shape[1])
    spread = lax.all_to_all(pieces, "seq", split_axis=0, concat_axis=0, tiled=True)
    ordered = jnp.take(spread, order, axis=0)
    gathered = lax.all_to_all(ordered, "seq", split_axis=0, concat_axis=0, tiled=True)
    return gathered.reshape(rows.shape)


def shards(cache, cache_len, group, group_req, req_order):
    factor = 1.0 / math.sqrt(HD)
    slot_of = inverse_table(req_order)
    index_of = inverse_table(group_req)
    query_source = jnp.take(index_of, req_order)
    cache_source = jnp.take(slot_of, group_req)
    me = lax.axis_index("seq")
    slot_request = jnp.take(req_order, me)
    slot_length = jnp.take(cache_len, slot_request)
    row_count = group.shape[2]
    feature_count = group.shape[3]
    head_count = feature_count // HD
    queries = group[0, 0]
    new_keys = group[1, 0].reshape(row_count, head_count, HD)
    new_values = group[2, 0].reshape(row_count, head_count, HD)
    local = lax.all_to_all(cache[:, 0], "tp", split_axis=2, concat_axis=1, tiled=True)
    position_count = local.shape[1]
    old_keys = local[0].reshape(position_count, head_count, HD)
    old_values = local[1].reshape(position_count, head_count, HD)
    slot_queries = permute_rows(queries, query_source).reshape(row_count, head_count, HD)
    live = (jnp.arange(position_count, dtype=jnp.int32) < slot_length)[None, :]
    top_c, sum_c, mixed_c = partial_part(slot_queries, old_keys, old_values, live, factor)
    packed = jnp.concatenate(
        [
            jnp.transpose(mixed_c, (1, 0, 2)).reshape(row_count, feature_count),
            jnp.transpose(top_c),
            jnp.transpose(sum_c),
        ],
        axis=1,
    )
    back = permute_rows(packed, cache_source)
    cache_part = (
        jnp.transpose(back[:, feature_count : feature_count + head_count]),
        jnp.transpose(back[:, feature_count + head_count :]),
        jnp.transpose(back[:, :feature_count].reshape(row_count, head_count, HD), (1, 0, 2)),
    )
    causal = (
        jnp.arange(row_count, dtype=jnp.int32)[:, None]
        >= jnp.arange(row_count, dtype=jnp.int32)[None, :]
    )
    group_part = partial_part(
        queries.reshape(row_count, head_count, HD), new_keys, new_values, causal, factor
    )
    context = combine_parts(cache_part, group_part)
    return context[None]


def solution(mesh):
    in_specs = (P(None, "seq", "tp", None), P(), P(None, "seq", None, "tp"), P(), P())
    out_specs = P("seq", None, "tp")
    return jax.shard_map(shards, mesh=mesh, in_specs=in_specs, out_specs=out_specs, check_vma=False)
```

profile of v0, /device:TPU:8, one launch (start us, length us, event | category | flops | bytes accessed | tf_op | source)
XLA Modules:
  0.0 167.5 jit_solution(6261947117886503793)
XLA Ops:
  0.0 1.9 %fusion.18 = (bf16[1,1,256,384]{3,2,1,0:T(8,128)(2,1)}, bf16[1,1,256,384]{3,2,1,0:T(8,128)(2,1)S(1)}, bf16[1,1,256,384]{3,2,1,0:T(8,128)(2,1)S(1)}) fusion(bf16[3,1,256,384]{3,2,1,0:T(8,128)(2,1)} %param.9), kind=kLoop, calls=%fused_computation.52 | loop fusion | bytes 1179648 | tf_op jit(solution)/shard_map/slice | solution.py:63
  1.9 0.7 reshape_squeeze.18
  2.7 18.9 %all-to-all-start = ((bf16[64,4,384]{2,1,0:T(4,128)(2,1)}), bf16[64,4,384]{2,1,0:T(4,128)(2,1)}, u32[]{:S(2)}, u32[]{:S(2)}) async-start(bf16[64,4,384]{2,1,0:T(4,128)(2,1)} %reshape_squeeze.18), calls=%async_computation | async-start | bytes 393216 | tf_op jit(solution)/shard_map/all_to_all | solution.py:44
  21.6 1.9 %copy.45 = bf16[2,1,64,3072]{2,0,3,1:T(2,128)(2,1)S(1)} copy(bf16[2,1,64,3072]{3,2,1,0:T(8,128)(2,1)S(1)} %copy-done.1) | data formatting | bytes 1572864 | tf_op args[0]
  23.5 1.1 bitcast_bitcast_fusion
  24.7 1.9 %reshape.168 = bf16[8,2,24576]{2,1,0:T(2,128)(2,1)} reshape(bf16[3072,2,64]{2,1,0:T(2,128)(2,1)S(1)} %bitcast_bitcast_fusion) | data formatting | bytes 1572864
  26.6 14.0 %all-to-all-done = bf16[64,4,384]{2,1,0:T(4,128)(2,1)} async-done(((bf16[64,4,384]{2,1,0:T(4,128)(2,1)}), bf16[64,4,384]{2,1,0:T(4,128)(2,1)}, u32[]{:S(2)}, u32[]{:S(2)}) %all-to-all-start) | async-done | bytes 196640 | tf_op jit(solution)/shard_map/all_to_all | solution.py:44
  40.6 4.3 %all-to-all-start.2 = ((bf16[8,2,24576]{2,1,0:T(2,128)(2,1)}), bf16[8,2,24576]{2,1,0:T(2,128)(2,1)S(1)}, u32[]{:S(2)}, u32[]{:S(2)}) async-start(bf16[8,2,24576]{2,1,0:T(2,128)(2,1)} %reshape.168), calls=%async_computation.2 | async-start | bytes 1572864 | tf_op jit(solution)/shard_map/all_to_all | solution.py:65
  45.0 0.8 gather_fusion.3
  45.8 1.7 %gather_fusion = bf16[64,4,384]{2,1,0:T(4,128)(2,1)S(1)} fusion(bf16[64,4,384]{2,1,0:T(4,128)(2,1)} %all-to-all-done, s32[1024]{0:T(1024)S(1)} %pad_clamp_fusion.1), kind=kCustom, calls=%fused_computation.2 | custom fusion | bytes 393472 | tf_op jit(solution)/shard_map/jit(_take)/gather | solution.py:45
  47.5 0.9 broadcast_select_fusion.1
  48.4 9.6 %all-to-all-done.2 = bf16[8,2,24576]{2,1,0:T(2,128)(2,1)S(1)} async-done(((bf16[8,2,24576]{2,1,0:T(2,128)(2,1)}), bf16[8,2,24576]{2,1,0:T(2,128)(2,1)S(1)}, u32[]{:S(2)}, u32[]{:S(2)}) %all-to-all-start.2) | async-done | bytes 786464 | tf_op jit(solution)/shard_map/all_to_all | solution.py:65
  58.0 6.4 %all-to-all-start.1 = ((bf16[64,4,384]{2,1,0:T(4,128)(2,1)}), bf16[64,4,384]{2,1,0:T(4,128)(2,1)}, u32[]{:S(2)}, u32[]{:S(2)}) async-start(bf16[64,4,384]{2,1,0:T(4,128)(2,1)} %broadcast_select_fusion.1), calls=%async_computation.1 | async-start | bytes 393216 | tf_op jit(solution)/shard_map/all_to_all | solution.py:46
  64.4 0.7 dynamic-slice.4
  65.8 0.7 dynamic-slice.5
  67.2 1.0 reshape.169
  68.2 1.2 copy.46
  70.2 13.6 %all-to-all-done.1 = bf16[64,4,384]{2,1,0:T(4,128)(2,1)} async-done(((bf16[64,4,384]{2,1,0:T(4,128)(2,1)}), bf16[64,4,384]{2,1,0:T(4,128)(2,1)}, u32[]{:S(2)}, u32[]{:S(2)}) %all-to-all-start.1) | async-done | bytes 196640 | tf_op jit(solution)/shard_map/all_to_all | solution.py:46
  83.8 1.1 reshape_reshape.3
  85.0 0.5 fusion
  85.5 0.6 convert_reduce_fusion
  86.1 0.7 convolution_bitcast_fusion.1
  87.1 0.4 concatenate.10
  87.8 1.0 pad_maximum_fusion
  88.8 5.5 %all-to-all-start.3 = ((f32[64,4,392]{2,1,0:T(4,128)}), f32[64,4,392]{2,1,0:T(4,128)S(1)}, u32[]{:S(2)}, u32[]{:S(2)}) async-start(f32[64,4,392]{2,1,0:T(4,128)} %pad_maximum_fusion), calls=%async_computation.3 | async-start | bytes 1048576 | tf_op jit(solution)/shard_map/all_to_all | solution.py:44
  94.4 0.8 gather_fusion.2
  95.3 30.8 %all-to-all-done.3 = f32[64,4,392]{2,1,0:T(4,128)S(1)} async-done(((f32[64,4,392]{2,1,0:T(4,128)}), f32[64,4,392]{2,1,0:T(4,128)S(1)}, u32[]{:S(2)}, u32[]{:S(2)}) %all-to-all-start.3) | async-done | bytes 401440 | tf_op jit(solution)/shard_map/all_to_all | solution.py:44
  126.0 0.9 gather_fusion.1
  126.9 1.0 broadcast_select_fusion
  127.9 6.0 %all-to-all-start.4 = ((f32[64,4,392]{2,1,0:T(4,128)}), f32[64,4,392]{2,1,0:T(4,128)S(1)}, u32[]{:S(2)}, u32[]{:S(2)}) async-start(f32[64,4,392]{2,1,0:T(4,128)} %broadcast_select_fusion), calls=%async_computation.4 | async-start | bytes 1048576 | tf_op jit(solution)/shard_map/all_to_all | solution.py:46
  134.9 30.8 %all-to-all-done.4 = f32[64,4,392]{2,1,0:T(4,128)S(1)} async-done(((f32[64,4,392]{2,1,0:T(4,128)}), f32[64,4,392]{2,1,0:T(4,128)S(1)}, u32[]{:S(2)}, u32[]{:S(2)}) %all-to-all-start.4) | async-done | bytes 401440 | tf_op jit(solution)/shard_map/all_to_all | solution.py:46
  166.7 0.8 copy.60
  (41 shorter events, 3.6 us)
Async XLA Ops:
  0.0 21.6 %copy-start.1 = (bf16[2,1,64,3072]{3,2,1,0:T(8,128)(2,1)S(1)}, bf16[2,1,64,3072]{3,2,1,0:T(8,128)(2,1)}, u32[]{:S(2)}) copy-start(bf16[2,1,64,3072]{3,2,1,0:T(8,128)(2,1)} %param.7) | copy-start | bytes 2359300
  2.7 37.9 %all-to-all-start = ((bf16[64,4,384]{2,1,0:T(4,128)(2,1)}), bf16[64,4,384]{2,1,0:T(4,128)(2,1)}, u32[]{:S(2)}, u32[]{:S(2)}) async-start(bf16[64,4,384]{2,1,0:T(4,128)(2,1)} %reshape_squeeze.18), calls=%async_computation | async-start | bytes 393216 | tf_op jit(solution)/shard_map/all_to_all | solution.py:44
  23.5 3.1 %copy-start.2 = (s32[64]{0:T(128)S(1)}, s32[64]{0:T(128)}, u32[]{:S(2)}) copy-start(s32[64]{0:T(128)} %param.11) | copy-start | bytes 772
  24.7 20.2 %copy-start.3 = (s32[64]{0:T(128)S(1)}, s32[64]{0:T(128)}, u32[]{:S(2)}) copy-start(s32[64]{0:T(128)} %param.10) | copy-start | bytes 772
  26.6 39.2 %copy-start.4 = (s32[64]{0:T(128)S(1)}, s32[64]{0:T(128)}, u32[]{:S(2)}) copy-start(s32[64]{0:T(128)} %param.8) | copy-start | bytes 772
  40.6 17.4 %all-to-all-start.2 = ((bf16[8,2,24576]{2,1,0:T(2,128)(2,1)}), bf16[8,2,24576]{2,1,0:T(2,128)(2,1)S(1)}, u32[]{:S(2)}, u32[]{:S(2)}) async-start(bf16[8,2,24576]{2,1,0:T(2,128)(2,1)} %reshape.168), calls=%async_computation.2 | async-start | bytes 1572864 | tf_op jit(solution)/shard_map/all_to_all | solution.py:65
  58.0 25.8 %all-to-all-start.1 = ((bf16[64,4,384]{2,1,0:T(4,128)(2,1)}), bf16[64,4,384]{2,1,0:T(4,128)(2,1)}, u32[]{:S(2)}, u32[]{:S(2)}) async-start(bf16[64,4,384]{2,1,0:T(4,128)(2,1)} %broadcast_select_fusion.1), calls=%async_computation.1 | async-start | bytes 393216 | tf_op jit(solution)/shard_map/all_to_all | solution.py:46
  88.8 37.3 %all-to-all-start.3 = ((f32[64,4,392]{2,1,0:T(4,128)}), f32[64,4,392]{2,1,0:T(4,128)S(1)}, u32[]{:S(2)}, u32[]{:S(2)}) async-start(f32[64,4,392]{2,1,0:T(4,128)} %pad_maximum_fusion), calls=%async_computation.3 | async-start | bytes 1048576 | tf_op jit(solution)/shard_map/all_to_all | solution.py:44
  94.3 39.7 %copy-start = (bf16[1,1,256,384]{3,2,1,0:T(8,128)(2,1)S(1)}, bf16[1,1,256,384]{3,2,1,0:T(8,128)(2,1)}, u32[]{:S(2)}) copy-start(bf16[1,1,256,384]{3,2,1,0:T(8,128)(2,1)} %get-tuple-element.37) | copy-start | bytes 589828
  127.9 37.8 %all-to-all-start.4 = ((f32[64,4,392]{2,1,0:T(4,128)}), f32[64,4,392]{2,1,0:T(4,128)S(1)}, u32[]{:S(2)}, u32[]{:S(2)}) async-start(f32[64,4,392]{2,1,0:T(4,128)} %broadcast_select_fusion), calls=%async_computation.4 | async-start | bytes 1048576 | tf_op jit(solution)/shard_map/all_to_all | solution.py:46
where the time goes:
time: 168 us
  waiting for transfers between devices  98.8 us (59%)
  starting transfers between devices  41.1 us (24%)
  local copies, waits for them, and re-layouts  20.1 us (12%)
  other arithmetic  3.87 us (2%)
  matrix products  1.95 us (1%)
  between operations  1.72 us (1%)
    all_to_all x2, waiting for transfers between devices, permute_rows(): lax.all_to_all(pieces, 'seq', split_axis=0, concat_axis=0, tiled=True)  44.7 us
    all_to_all x2, waiting for transfers between devices, permute_rows(): lax.all_to_all(ordered, 'seq', split_axis=0, concat_axis=0, tiled=True)  44.5 us
    all_to_all x2, starting transfers between devices, permute_rows(): lax.all_to_all(pieces, 'seq', split_axis=0, concat_axis=0, tiled=True)  24.4 us
    all_to_all x2, starting transfers between devices, permute_rows(): lax.all_to_all(ordered, 'seq', split_axis=0, concat_axis=0, tiled=True)  12.4 us
    all_to_all x1, waiting for transfers between devices, shards(): lax.all_to_all(cache[:, 0], 'tp', split_axis=2, concat_axis=1, tiled=True)  9.63 us
    unnamed x16, local copies, waits for them, and re-layouts  6.19 us
    all_to_all x1, starting transfers between devices, shards(): lax.all_to_all(cache[:, 0], 'tp', split_axis=2, concat_axis=1, tiled=True)  4.3 us
  transfers between devices with their start and end apart: 5, of which 5 were waited for; matrix products, arithmetic and copies ran while one was open for 9% of the time, Pallas kernels for 0%

commit v1 on v0

--- a/solution.py
+++ b/solution.py
@@ -5,6 +5,22 @@
 from jax.sharding import PartitionSpec as P
 
 HD = 96
+
+
+def swapped_with_each(x, axis, split, join):
+    ways, here = (lax.axis_size(axis), lax.axis_index(axis))
+    width = x.shape[split] // ways
+    lengths = list(x.shape)
+    lengths[split] = width
+    height = lengths[join]
+    lengths[join] = height * ways
+    full = jnp.zeros(lengths, x.dtype)
+    for mask in range(ways):
+        part = lax.dynamic_slice_in_dim(x, (here ^ mask) * width, width, axis=split)
+        if mask:
+            part = lax.ppermute(part, axis, [(d, d ^ mask) for d in range(ways)])
+        full = lax.dynamic_update_slice_in_dim(full, part, (here ^ mask) * height, axis=join)
+    return full
 
 
 def inverse_table(permutation):
@@ -62,7 +78,7 @@
     queries = group[0, 0]
     new_keys = group[1, 0].reshape(row_count, head_count, HD)
     new_values = group[2, 0].reshape(row_count, head_count, HD)
-    local = lax.all_to_all(cache[:, 0], "tp", split_axis=2, concat_axis=1, tiled=True)
+    local = swapped_with_each(cache[:, 0], "tp", 2, 1)
     position_count = local.shape[1]
     old_keys = local[0].reshape(position_count, head_count, HD)
     old_values = local[1].reshape(position_count, head_count, HD)

time: 168 us -> 177 us (1.054)
  the two profiles are of different devices: /device:TPU:8 before, /device:TPU:6 now
where the time goes in v1:
time: 177 us; the launch traced here: 176 us
  waiting for transfers between devices  80 us (45%)
  starting transfers between devices  66.7 us (38%)
  local copies, waits for them, and re-layouts  20.9 us (12%)
  other arithmetic  5.2 us (3%)
  matrix products  1.86 us (1%)
  between operations  1.86 us (1%)
    all_to_all x2, waiting for transfers between devices, permute_rows(): lax.all_to_all(pieces, 'seq', split_axis=0, concat_axis=0, tiled=True)  48.9 us
    all_to_all x2, starting transfers between devices, permute_rows(): lax.all_to_all(pieces, 'seq', split_axis=0, concat_axis=0, tiled=True)  34 us
    all_to_all x2, waiting for transfers between devices, permute_rows(): lax.all_to_all(ordered, 'seq', split_axis=0, concat_axis=0, tiled=True)  31 us
    ppermute x7, starting transfers between devices, swapped_with_each(): part = lax.ppermute(part, axis, [(d, d ^ mask) for d in range(ways)])  22.3 us
    all_to_all x2, starting transfers between devices, permute_rows(): lax.all_to_all(ordered, 'seq', split_axis=0, concat_axis=0, tiled=True)  10.5 us
    dynamic_update_slice x8, local copies, waits for them, and re-layouts, swapped_with_each(): lax.dynamic_update_slice_in_dim(full, part, (here ^ mask) * height, axis=...  9.79 us
  transfers between devices with their start and end apart: 11, of which 3 were waited for; matrix products, arithmetic and copies ran while one was open for 10% of the time, Pallas kernels for 0%

profile of v1, /device:TPU:6, one launch (start us, length us, event | category | flops | bytes accessed | tf_op | source)
XLA Modules:
  0.0 176.4 jit_solution(7213443276418190235)
XLA Ops:
  0.0 1.2 fusion.16
  1.3 0.7 reshape_squeeze.18
  2.0 18.9 %all-to-all-start = ((bf16[64,4,384]{2,1,0:T(4,128)(2,1)}), bf16[64,4,384]{2,1,0:T(4,128)(2,1)S(1)}, u32[]{:S(2)}, u32[]{:S(2)}) async-start(bf16[64,4,384]{2,1,0:T(4,128)(2,1)} %reshape_squeeze.18), calls=%async_computation | async-start | bytes 393216 | tf_op jit(solution)/shard_map/all_to_all | solution.py:60
  21.5 0.8 select_reduce_fusion
  22.3 0.8 gather_fusion.3
  23.1 17.9 %all-to-all-done = bf16[64,4,384]{2,1,0:T(4,128)(2,1)S(1)} async-done(((bf16[64,4,384]{2,1,0:T(4,128)(2,1)}), bf16[64,4,384]{2,1,0:T(4,128)(2,1)S(1)}, u32[]{:S(2)}, u32[]{:S(2)}) %all-to-all-start) | async-done | bytes 196640 | tf_op jit(solution)/shard_map/all_to_all | solution.py:60
  41.1 0.8 gather_fusion
  41.8 0.9 broadcast_select_fusion.1
  42.7 4.6 %all-to-all-start.1 = ((bf16[64,4,384]{2,1,0:T(4,128)(2,1)}), bf16[64,4,384]{2,1,0:T(4,128)(2,1)S(1)}, u32[]{:S(2)}, u32[]{:S(2)}) async-start(bf16[64,4,384]{2,1,0:T(4,128)(2,1)} %broadcast_select_fusion.1), calls=%async_computation.1 | async-start | bytes 393216 | tf_op jit(solution)/shard_map/all_to_all | solution.py:62
  47.5 1.9 %collective-permute-start = (bf16[2,64,384]{2,1,0:T(8,128)(2,1)S(1)}, bf16[2,64,384]{2,1,0:T(8,128)(2,1)S(1)}, u32[]{:S(2)}, u32[]{:S(2)}) collective-permute-start(bf16[2,64,384]{2,1,0:T(8,128)(2,1)S(1)} %get-tuple-element.43), channel_id=1, source_target_pairs={{0,1},{1,0},{2,3},{3,2},{4,5},{5,4},{6,7},{7,6},{8,9},{9,8},{10,11... | collective-permute-start | bytes 294920 | tf_op jit(solution)/shard_map/ppermute | solution.py:21
  49.5 2.7 %collective-permute-start.1 = (bf16[2,64,384]{2,1,0:T(8,128)(2,1)S(1)}, bf16[2,64,384]{2,1,0:T(8,128)(2,1)S(1)}, u32[]{:S(2)}, u32[]{:S(2)}) collective-permute-start(bf16[2,64,384]{2,1,0:T(8,128)(2,1)S(1)} %get-tuple-element.42), channel_id=1, source_target_pairs={{0,2},{1,3},{2,0},{3,1},{4,6},{5,7},{6,4},{7,5},{8,10},{9,11},{10,... | collective-permute-start | bytes 294920 | tf_op jit(solution)/shard_map/ppermute | solution.py:21
  52.2 2.9 %collective-permute-start.2 = (bf16[2,64,384]{2,1,0:T(8,128)(2,1)S(1)}, bf16[2,64,384]{2,1,0:T(8,128)(2,1)S(1)}, u32[]{:S(2)}, u32[]{:S(2)}) collective-permute-start(bf16[2,64,384]{2,1,0:T(8,128)(2,1)S(1)} %get-tuple-element.41), channel_id=1, source_target_pairs={{0,3},{1,2},{2,1},{3,0},{4,7},{5,6},{6,5},{7,4},{8,11},{9,10},{10,... | collective-permute-start | bytes 294920 | tf_op jit(solution)/shard_map/ppermute | solution.py:21
  55.1 3.3 %collective-permute-start.3 = (bf16[2,64,384]{2,1,0:T(8,128)(2,1)S(1)}, bf16[2,64,384]{2,1,0:T(8,128)(2,1)S(1)}, u32[]{:S(2)}, u32[]{:S(2)}) collective-permute-start(bf16[2,64,384]{2,1,0:T(8,128)(2,1)S(1)} %get-tuple-element.40), channel_id=1, source_target_pairs={{0,4},{1,5},{2,6},{3,7},{4,0},{5,1},{6,2},{7,3},{8,12},{9,13},{10,... | collective-permute-start | bytes 294920 | tf_op jit(solution)/shard_map/ppermute | solution.py:21
  58.5 3.7 %collective-permute-start.4 = (bf16[2,64,384]{2,1,0:T(8,128)(2,1)S(1)}, bf16[2,64,384]{2,1,0:T(8,128)(2,1)S(1)}, u32[]{:S(2)}, u32[]{:S(2)}) collective-permute-start(bf16[2,64,384]{2,1,0:T(8,128)(2,1)S(1)} %get-tuple-element.39), channel_id=1, source_target_pairs={{0,5},{1,4},{2,7},{3,6},{4,1},{5,0},{6,3},{7,2},{8,13},{9,12},{10,... | collective-permute-start | bytes 294920 | tf_op jit(solution)/shard_map/ppermute | solution.py:21
  65.6 2.6 %collective-permute-start.5 = (bf16[2,64,384]{2,1,0:T(8,128)(2,1)S(1)}, bf16[2,64,384]{2,1,0:T(8,128)(2,1)S(1)}, u32[]{:S(2)}, u32[]{:S(2)}) collective-permute-start(bf16[2,64,384]{2,1,0:T(8,128)(2,1)S(1)} %get-tuple-element.38), channel_id=1, source_target_pairs={{0,6},{1,7},{2,4},{3,5},{4,2},{5,3},{6,0},{7,1},{8,14},{9,15},{10,... | collective-permute-start | bytes 294920 | tf_op jit(solution)/shard_map/ppermute | solution.py:21
  68.3 5.1 %collective-permute-start.6 = (bf16[2,64,384]{2,1,0:T(8,128)(2,1)S(1)}, bf16[2,64,384]{2,1,0:T(8,128)(2,1)S(1)}, u32[]{:S(2)}, u32[]{:S(2)}) collective-permute-start(bf16[2,64,384]{2,1,0:T(8,128)(2,1)S(1)} %get-tuple-element.37), channel_id=1, source_target_pairs={{0,7},{1,6},{2,5},{3,4},{4,3},{5,2},{6,1},{7,0},{8,15},{9,14},{10,... | collective-permute-start | bytes 294920 | tf_op jit(solution)/shard_map/ppermute | solution.py:21
  73.6 1.4 dynamic_update_slice.25
  75.2 0.9 dynamic_update_slice.26
  76.3 1.6 dynamic_update_slice.27
  78.1 0.9 dynamic_update_slice.28
  79.3 1.6 dynamic_update_slice.29
  81.1 0.9 dynamic_update_slice.30
  82.2 1.6 dynamic_update_slice.31
  86.9 1.0 pad_maximum_fusion
  87.9 15.1 %all-to-all-start.2 = ((f32[64,4,392]{2,1,0:T(4,128)}), f32[64,4,392]{2,1,0:T(4,128)S(1)}, u32[]{:S(2)}, u32[]{:S(2)}) async-start(f32[64,4,392]{2,1,0:T(4,128)} %pad_maximum_fusion), calls=%async_computation.2 | async-start | bytes 1048576 | tf_op jit(solution)/shard_map/all_to_all | solution.py:60
  103.1 0.8 gather_fusion.2
  103.9 31.0 %all-to-all-done.2 = f32[64,4,392]{2,1,0:T(4,128)S(1)} async-done(((f32[64,4,392]{2,1,0:T(4,128)}), f32[64,4,392]{2,1,0:T(4,128)S(1)}, u32[]{:S(2)}, u32[]{:S(2)}) %all-to-all-start.2) | async-done | bytes 401440 | tf_op jit(solution)/shard_map/all_to_all | solution.py:60
  134.9 0.9 gather_fusion.1
  135.8 1.0 broadcast_select_fusion
  136.7 5.8 %all-to-all-start.3 = ((f32[64,4,392]{2,1,0:T(4,128)}), f32[64,4,392]{2,1,0:T(4,128)S(1)}, u32[]{:S(2)}, u32[]{:S(2)}) async-start(f32[64,4,392]{2,1,0:T(4,128)} %broadcast_select_fusion), calls=%async_computation.3 | async-start | bytes 1048576 | tf_op jit(solution)/shard_map/all_to_all | solution.py:62
  143.6 31.0 %all-to-all-done.3 = f32[64,4,392]{2,1,0:T(4,128)S(1)} async-done(((f32[64,4,392]{2,1,0:T(4,128)}), f32[64,4,392]{2,1,0:T(4,128)S(1)}, u32[]{:S(2)}, u32[]{:S(2)}) %all-to-all-start.3) | async-done | bytes 401440 | tf_op jit(solution)/shard_map/all_to_all | solution.py:62
  175.6 0.8 copy.96
  (61 shorter events, 9.3 us)
Async XLA Ops:
  0.0 23.1 %copy-start.1 = (s32[64]{0:T(128)S(1)}, s32[64]{0:T(128)}, u32[]{:S(2)}) copy-start(s32[64]{0:T(128)} %param.11) | copy-start | bytes 772
  0.0 47.4 %copy-start = (bf16[2,1,64,3072]{3,2,1,0:T(8,128)(2,1)S(1)}, bf16[2,1,64,3072]{3,2,1,0:T(8,128)(2,1)}, u32[]{:S(2)}) copy-start(bf16[2,1,64,3072]{3,2,1,0:T(8,128)(2,1)} %param.7) | copy-start | bytes 2359300
  2.0 61.6 %copy-start.3 = (s32[64]{0:T(128)S(1)}, s32[64]{0:T(128)}, u32[]{:S(2)}) copy-start(s32[64]{0:T(128)} %param.8) | copy-start | bytes 772
  2.0 39.1 %all-to-all-start = ((bf16[64,4,384]{2,1,0:T(4,128)(2,1)}), bf16[64,4,384]{2,1,0:T(4,128)(2,1)S(1)}, u32[]{:S(2)}, u32[]{:S(2)}) async-start(bf16[64,4,384]{2,1,0:T(4,128)(2,1)} %reshape_squeeze.18), calls=%async_computation | async-start | bytes 393216 | tf_op jit(solution)/shard_map/all_to_all | solution.py:60
  42.7 41.2 %all-to-all-start.1 = ((bf16[64,4,384]{2,1,0:T(4,128)(2,1)}), bf16[64,4,384]{2,1,0:T(4,128)(2,1)S(1)}, u32[]{:S(2)}, u32[]{:S(2)}) async-start(bf16[64,4,384]{2,1,0:T(4,128)(2,1)} %broadcast_select_fusion.1), calls=%async_computation.1 | async-start | bytes 393216 | tf_op jit(solution)/shard_map/all_to_all | solution.py:62
  47.5 18.1 %collective-permute-start = (bf16[2,64,384]{2,1,0:T(8,128)(2,1)S(1)}, bf16[2,64,384]{2,1,0:T(8,128)(2,1)S(1)}, u32[]{:S(2)}, u32[]{:S(2)}) collective-permute-start(bf16[2,64,384]{2,1,0:T(8,128)(2,1)S(1)} %get-tuple-element.43), channel_id=1, source_target_pairs={{0,1},{1,0},{2,3},{3,2},{4,5},{5,4},{6,7},{7,6},{8,9},{9,8},{10,11... | collective-permute-start | bytes 294920 | tf_op jit(solution)/shard_map/ppermute | solution.py:21
  49.5 18.8 %collective-permute-start.1 = (bf16[2,64,384]{2,1,0:T(8,128)(2,1)S(1)}, bf16[2,64,384]{2,1,0:T(8,128)(2,1)S(1)}, u32[]{:S(2)}, u32[]{:S(2)}) collective-permute-start(bf16[2,64,384]{2,1,0:T(8,128)(2,1)S(1)} %get-tuple-element.42), channel_id=1, source_target_pairs={{0,2},{1,3},{2,0},{3,1},{4,6},{5,7},{6,4},{7,5},{8,10},{9,11},{10,... | collective-permute-start | bytes 294920 | tf_op jit(solution)/shard_map/ppermute | solution.py:21
  52.2 23.9 %collective-permute-start.2 = (bf16[2,64,384]{2,1,0:T(8,128)(2,1)S(1)}, bf16[2,64,384]{2,1,0:T(8,128)(2,1)S(1)}, u32[]{:S(2)}, u32[]{:S(2)}) collective-permute-start(bf16[2,64,384]{2,1,0:T(8,128)(2,1)S(1)} %get-tuple-element.41), channel_id=1, source_target_pairs={{0,3},{1,2},{2,1},{3,0},{4,7},{5,6},{6,5},{7,4},{8,11},{9,10},{10,... | collective-permute-start | bytes 294920 | tf_op jit(solution)/shard_map/ppermute | solution.py:21
  55.1 22.8 %collective-permute-start.3 = (bf16[2,64,384]{2,1,0:T(8,128)(2,1)S(1)}, bf16[2,64,384]{2,1,0:T(8,128)(2,1)S(1)}, u32[]{:S(2)}, u32[]{:S(2)}) collective-permute-start(bf16[2,64,384]{2,1,0:T(8,128)(2,1)S(1)} %get-tuple-element.40), channel_id=1, source_target_pairs={{0,4},{1,5},{2,6},{3,7},{4,0},{5,1},{6,2},{7,3},{8,12},{9,13},{10,... | collective-permute-start | bytes 294920 | tf_op jit(solution)/shard_map/ppermute | solution.py:21
  58.5 20.6 %collective-permute-start.4 = (bf16[2,64,384]{2,1,0:T(8,128)(2,1)S(1)}, bf16[2,64,384]{2,1,0:T(8,128)(2,1)S(1)}, u32[]{:S(2)}, u32[]{:S(2)}) collective-permute-start(bf16[2,64,384]{2,1,0:T(8,128)(2,1)S(1)} %get-tuple-element.39), channel_id=1, source_target_pairs={{0,5},{1,4},{2,7},{3,6},{4,1},{5,0},{6,3},{7,2},{8,13},{9,12},{10,... | collective-permute-start | bytes 294920 | tf_op jit(solution)/shard_map/ppermute | solution.py:21
  65.6 15.3 %collective-permute-start.5 = (bf16[2,64,384]{2,1,0:T(8,128)(2,1)S(1)}, bf16[2,64,384]{2,1,0:T(8,128)(2,1)S(1)}, u32[]{:S(2)}, u32[]{:S(2)}) collective-permute-start(bf16[2,64,384]{2,1,0:T(8,128)(2,1)S(1)} %get-tuple-element.38), channel_id=1, source_target_pairs={{0,6},{1,7},{2,4},{3,5},{4,2},{5,3},{6,0},{7,1},{8,14},{9,15},{10,... | collective-permute-start | bytes 294920 | tf_op jit(solution)/shard_map/ppermute | solution.py:21
  68.3 13.8 %collective-permute-start.6 = (bf16[2,64,384]{2,1,0:T(8,128)(2,1)S(1)}, bf16[2,64,384]{2,1,0:T(8,128)(2,1)S(1)}, u32[]{:S(2)}, u32[]{:S(2)}) collective-permute-start(bf16[2,64,384]{2,1,0:T(8,128)(2,1)S(1)} %get-tuple-element.37), channel_id=1, source_target_pairs={{0,7},{1,6},{2,5},{3,4},{4,3},{5,2},{6,1},{7,0},{8,15},{9,14},{10,... | collective-permute-start | bytes 294920 | tf_op jit(solution)/shard_map/ppermute | solution.py:21
  86.2 17.7 %copy-start.2 = (s32[64]{0:T(128)S(1)}, s32[64]{0:T(128)}, u32[]{:S(2)}) copy-start(s32[64]{0:T(128)} %param.10) | copy-start | bytes 772
  87.9 47.0 %all-to-all-start.2 = ((f32[64,4,392]{2,1,0:T(4,128)}), f32[64,4,392]{2,1,0:T(4,128)S(1)}, u32[]{:S(2)}, u32[]{:S(2)}) async-start(f32[64,4,392]{2,1,0:T(4,128)} %pad_maximum_fusion), calls=%async_computation.2 | async-start | bytes 1048576 | tf_op jit(solution)/shard_map/all_to_all | solution.py:60
  136.7 37.9 %all-to-all-start.3 = ((f32[64,4,392]{2,1,0:T(4,128)}), f32[64,4,392]{2,1,0:T(4,128)S(1)}, u32[]{:S(2)}, u32[]{:S(2)}) async-start(f32[64,4,392]{2,1,0:T(4,128)} %broadcast_select_fusion), calls=%async_computation.3 | async-start | bytes 1048576 | tf_op jit(solution)/shard_map/all_to_all | solution.py:62
